TPU v7x, 32 devices: a whole 2x2x4 slice. The times are simulated.
32 devices in a mesh: groups: 2 (over y), blk: 4 (over z), pool: 4 (over x, core).
Axes of the slice: x: 2, y: 2, z: 4, core: 2. Of those that a mesh axis runs over, the one named last changes fastest.
Arguments:
- q_new: bfloat16 [1024, 8192], P(('groups', 'blk'), 'pool'), parts along dimension 0, may hold values from -64 to 64
- kv_new: bfloat16 [1024, 8, 256], P(('groups', 'blk'), 'pool'), parts along dimension 0, may hold values from -7 to 7
- kv_cache: bfloat16 [256, 8, 128, 256], P(('groups', 'blk'), 'pool'), parts along dimension 0, may hold values from -4.5 to 4.5
- page_table: int32 [16], P('groups'), parts along dimension 0, may hold values from 0 to 127, as said below
- block_offsets: int32 [8], P('groups'), parts along dimension 0, may hold values from 0 to 3, each once
Outputs:
- attended: bfloat16 [1024, 8192], P(('groups', 'blk'), 'pool'), parts along dimension 0
There are 2 independent parts, one for each index of `groups`. A program takes and returns all parts, laid end to end along the dimension named above; each array names one. Nothing has to cross between parts.
Inputs may be any that keep to these rules, and one draw needn't show every extreme that they name: `page_table`: distinct slots; slot s lies on blk index s // 32; at most 4 entries lie on the slots of one blk index, and exactly 4 on some blk index.
All inputs are finite; a program needn't handle non-finite values.
Results may differ from a plain program's by a relative error of at most 0.0045.
Values may be sent and summed in bfloat16 or wider, within the bound.
No kernel may reach another device: no remote copies, remote signals or barrier semaphores. Data moves between devices by JAX's collectives and lax.ppermute only.
A program may use at most 64 MiB of HBM per device.

v0:
```python
import math
import jax
import jax.numpy as jnp
from jax import lax
from jax.sharding import PartitionSpec as P

CAP = 4


def attend(running, queries, keys, values, visible, head_size):
    maxima, totals, summed = running
    score_scale = 1.0 / math.sqrt(head_size)
    scores = (
        jnp.einsum("gqd,gkd->gqk", queries, keys, preferred_element_type=jnp.float32) * score_scale
    )
    scores = jnp.where(visible, scores, -1e30)
    row_top = jnp.maximum(maxima, jnp.max(scores, axis=2))
    factor = jnp.exp(maxima - row_top)
    weights = jnp.where(visible, jnp.exp(scores - row_top[..., None]), 0.0)
    totals = totals * factor + jnp.sum(weights, axis=2)
    summed = summed * factor[..., None] + jnp.einsum(
        "gqk,gkd->gqd", weights.astype(jnp.bfloat16), values, preferred_element_type=jnp.float32
    )
    return (row_top, totals, summed)


def local(q_new, kv_new, kv_cache, page_table, block_offsets):
    q_rows = q_new.shape[0]
    kv_heads = kv_new.shape[1]
    head_size = kv_new.shape[2] // 2
    group_size = q_new.shape[1] // (head_size * kv_heads)
    slots_dev = kv_cache.shape[0]
    page_len = kv_cache.shape[2]
    npages = page_table.shape[0]
    blocks = lax.axis_size("blk")
    myself = lax.axis_index("blk")
    pg = -(-npages // blocks)
    block_ids = jnp.arange(blocks, dtype=jnp.int32)
    my_offset = jnp.sum(jnp.where(block_ids == myself, block_offsets, 0))
    query_pos = jnp.tile(my_offset * q_rows + jnp.arange(q_rows, dtype=jnp.int32), group_size)
    queries = (
        q_new.reshape(q_rows, kv_heads, group_size, head_size)
        .transpose(1, 2, 0, 3)
        .reshape(kv_heads, group_size * q_rows, head_size)
    )
    query_span = group_size * q_rows
    page_owner = page_table // slots_dev
    owned = page_owner == myself
    page_rank = jnp.cumsum(owned.astype(jnp.int32)) - 1
    local_slot = page_table % slots_dev
    counts = jnp.sum((page_owner[None, :] == block_ids[:, None]).astype(jnp.int32), axis=1)
    per_peer = (CAP + blocks - 1) // blocks
    starts = jnp.cumsum(counts) - counts
    my_start = jnp.sum(jnp.where(block_ids == myself, starts, 0))
    peer_slots = jnp.arange(per_peer, dtype=jnp.int32)[None, :]
    wanted = (block_ids[:, None] - my_start) % blocks + peer_slots * blocks
    picked = owned[None, None, :] & (page_rank[None, None, :] == wanted[..., None])
    chosen = jnp.sum(jnp.where(picked, local_slot[None, None, :], 0), axis=2).reshape(-1)
    sent_pages = kv_cache[chosen].reshape(blocks, per_peer, kv_heads, page_len, 2 * head_size)
    sent_pages = sent_pages.transpose(0, 2, 1, 3, 4).reshape(
        blocks, kv_heads, per_peer * page_len, 2 * head_size
    )
    own_rows = jnp.broadcast_to(
        kv_new.transpose(1, 0, 2)[None], (blocks, kv_heads, q_rows, 2 * head_size)
    )
    payload = jnp.concatenate([sent_pages, own_rows], axis=2)
    received = lax.all_to_all(payload, "blk", split_axis=0, concat_axis=0, tiled=True)
    page_part = received[:, :, : per_peer * page_len]
    page_part = page_part.reshape(blocks, kv_heads, per_peer, page_len, 2 * head_size)
    page_part = page_part.transpose(0, 2, 1, 3, 4).reshape(
        blocks * per_peer, kv_heads, page_len, 2 * head_size
    )
    arriving = (myself - starts[:, None]) % blocks + peer_slots * blocks
    present = (arriving < counts[:, None]).reshape(-1)
    order_rank = jnp.cumsum(present.astype(jnp.int32)) - 1
    choose = present[None, :] & (order_rank[None, :] == jnp.arange(pg, dtype=jnp.int32)[:, None])
    positions = jnp.sum(
        jnp.where(choose, jnp.arange(blocks * per_peer, dtype=jnp.int32)[None, :], 0), axis=1
    )
    compact = page_part[positions]
    compact_valid = jnp.arange(pg, dtype=jnp.int32) * blocks + myself < npages
    gathered = lax.all_gather(compact, "blk", axis=0, tiled=True)
    gathered_valid = (
        jnp.arange(pg, dtype=jnp.int32)[None, :] * blocks + block_ids[:, None] < npages
    ).reshape(-1)
    new_rows = received[:, :, per_peer * page_len :]
    new_rows = new_rows.transpose(1, 0, 2, 3).reshape(kv_heads, blocks * q_rows, 2 * head_size)
    own_pages = compact.transpose(1, 0, 2, 3).reshape(kv_heads, pg * page_len, 2 * head_size)
    entries_a = jnp.concatenate([new_rows, own_pages], axis=1)
    row_source = jnp.repeat(block_ids, q_rows)
    key_pos = jnp.sum(
        jnp.where(row_source[:, None] == block_ids[None, :], block_offsets[None, :], 0), axis=1
    ) * q_rows + jnp.tile(jnp.arange(q_rows, dtype=jnp.int32), blocks)
    visible_new = key_pos[None, :] <= query_pos[:, None]
    visible_own = jnp.broadcast_to(
        jnp.repeat(compact_valid, page_len)[None, :], (query_span, pg * page_len)
    )
    visible_a = jnp.concatenate([visible_new, visible_own], axis=1)[None]
    running = (
        jnp.full((kv_heads, query_span), -1e30, jnp.float32),
        jnp.zeros((kv_heads, query_span), jnp.float32),
        jnp.zeros((kv_heads, query_span, head_size), jnp.float32),
    )
    running = attend(
        running,
        queries,
        entries_a[..., :head_size],
        entries_a[..., head_size:],
        visible_a,
        head_size,
    )
    page_block = jnp.repeat(block_ids, pg)
    use_page = gathered_valid & (page_block != myself)
    entries_b = gathered.transpose(1, 0, 2, 3).reshape(
        kv_heads, blocks * pg * page_len, 2 * head_size
    )
    visible_b = jnp.repeat(use_page, page_len)[None, None, :]
    running = attend(
        running,
        queries,
        entries_b[..., :head_size],
        entries_b[..., head_size:],
        visible_b,
        head_size,
    )
    maxima, totals, summed = running
    attended = (summed / totals[..., None]).astype(jnp.bfloat16)
    attended = attended.reshape(kv_heads, group_size, q_rows, head_size).transpose(2, 0, 1, 3)
    return attended.reshape(q_rows, kv_heads * group_size * head_size)


def solution(mesh):
    return jax.shard_map(
        local,
        mesh=mesh,
        in_specs=(
            P(("groups", "blk"), "pool"),
            P(("groups", "blk"), "pool", None),
            P(("groups", "blk"), "pool", None, None),
            P("groups"),
            P("groups"),
        ),
        out_specs=P(("groups", "blk"), "pool"),
        check_vma=False,
    )
```

profile of v0, /device:TPU:0, one launch (start us, length us, event | category | flops | bytes accessed | tf_op | source)
XLA Modules:
  0.0 97.5 jit_solution(11759745901006424764)
XLA Ops:
  6.5 0.0 copy-start.1
  6.5 0.0 copy-start
  6.5 0.7 and_select_fusion.3
  7.3 0.7 convert_bitcast_fusion
  7.9 0.2 reduce-window.21
  8.1 0.1 convert_reduce_fusion
  8.2 0.2 reduce-window.22
  8.4 1.4 %fusion.35 = (s32[]{:T(128)}, s32[]{:T(128)}) fusion(s32[4]{0:T(128)} %param.9, s32[]{:T(128)S(6)} %axis_index.15, s32[4]{0:T(128)S(1)} %convert_reduce_fusion, s32[4,1]{0,1:T(1,128)S(1)} %reduce-window.22), kind=kLoop, calls=%fused_computation.78 | loop fusion | flops 22 | bytes 60 | tf_op jit(solution)/shard_map/reduce_sum | solution.py:39
  9.8 0.7 and_select_fusion.4
  10.5 0.2 select_reduce_fusion.1
  10.7 0.9 copy.22
  11.6 2.8 %gather_fusion = bf16[4,2,128,256]{3,2,1,0:T(8,128)(2,1)S(1)} fusion(bf16[32,2,128,256]{3,2,1,0:T(8,128)(2,1)} %param.7, s32[1024]{0:T(1024)S(1)} %pad_clamp_fusion.1), kind=kCustom, calls=%fused_computation | custom fusion | bytes 1048592 | tf_op jit(solution)/shard_map/gather | solution.py:59
  14.4 1.1 %pad_maximum_fusion = bf16[4,2,256,256]{3,2,1,0:T(8,128)(2,1)} fusion(bf16[4,2,128,256]{3,2,1,0:T(8,128)(2,1)S(1)} %broadcast_in_dim.150, bf16[4,2,128,256]{3,2,1,0:T(8,128)(2,1)S(1)} %gather_fusion), kind=kLoop, calls=%fused_computation.23 | loop fusion | flops 2097152 | bytes 2097152 | tf_op jit(solution)/shard_map/concatenate | solution.py:66
  15.5 6.3 %all-to-all-start = ((bf16[4,2,256,256]{3,2,1,0:T(8,128)(2,1)}), bf16[4,2,256,256]{3,2,1,0:T(8,128)(2,1)S(1)}, u32[]{:S(2)}, u32[]{:S(2)}) async-start(bf16[4,2,256,256]{3,2,1,0:T(8,128)(2,1)} %pad_maximum_fusion), calls=%async_computation | async-start | bytes 2097152 | tf_op jit(solution)/shard_map/all_to_all | solution.py:67
  21.8 0.0 all-gather.3.cloned.1.call-start
  21.9 0.1 and.99
  21.9 0.2 reduce-window.23
  22.1 0.0 copy-done
  22.1 0.1 copy.32
  22.2 0.1 copy.25
  22.4 0.1 broadcast_bitcast_fusion.2
  23.2 0.1 fusion.33
  23.3 0.0 copy-done.1
  23.3 0.1 select_reduce_fusion
  23.4 24.1 %all-to-all-done = bf16[4,2,256,256]{3,2,1,0:T(8,128)(2,1)S(1)} async-done(((bf16[4,2,256,256]{3,2,1,0:T(8,128)(2,1)}), bf16[4,2,256,256]{3,2,1,0:T(8,128)(2,1)S(1)}, u32[]{:S(2)}, u32[]{:S(2)}) %all-to-all-start) | async-done | bytes 1048608 | tf_op jit(solution)/shard_map/all_to_all | solution.py:67
  47.6 0.1 fusion.51
  47.7 1.3 %gather_fusion.1 = bf16[2,2,128,256]{3,2,1,0:T(8,128)(2,1)} fusion(bf16[4,2,128,256]{3,2,1,0:T(8,128)(2,1)S(1)} %get-tuple-element.10, s32[1024]{0:T(1024)S(1)} %pad_clamp_fusion), kind=kCustom, calls=%fused_computation.1 | custom fusion | bytes 524296 | tf_op jit(solution)/shard_map/gather | solution.py:80
  48.9 0.0 all-gather.3.cloned.1.call-update
  48.9 0.1 broadcast_bitcast_fusion.1
  49.0 0.4 broadcast_compare_fusion
  49.4 0.4 pad_add_fusion
  49.8 1.0 copy.24
  50.8 4.0 %fusion.4 = (f32[2,1024]{1,0:T(2,128)S(1)}, f32[2,768,1024]{2,1,0:T(8,128)}) fusion(pred[1024,768]{0,1:T(8,128)(4,1)S(1)} %pad_add_fusion, bf16[2,1024,128]{2,1,0:T(8,128)(2,1)S(1)} %bitcast.92, bf16[2,512,256]{2,1,0:T(8,128)(2,1)S(1)} %bitcast.98, bf16[2,256,256]{2,1,0:T(8,128)(2,1)S(1)} %bitcast.101), kind=kOutput, calls=%fused_computation.11 | convolution fusion | flops 408156160 | bytes 8396800 | tf_op jit(solution)/shard_map/gqd,gkd->gqk/dot_general | solution.py:14
  54.9 21.3 %all-gather.3.cloned.1.call-done = bf16[8,2,128,256]{3,2,1,0:T(8,128)(2,1)} async-done(((bf16[2,2,128,256]{3,2,1,0:T(8,128)(2,1)}), bf16[8,2,128,256]{3,2,1,0:T(8,128)(2,1)}) %all-gather.3.cloned.1.call-update) | async-done | bytes 1048592 | tf_op jit(solution)/shard_map/all_gather | solution.py:82
  76.1 1.3 %copy.27 = bf16[2,8,128,256]{3,2,1,0:T(8,128)(2,1)S(1)} copy(bf16[2,8,128,256]{3,2,0,1:T(8,128)(2,1)} %bitcast.96) | data formatting | bytes 2097152 | tf_op jit(solution)/shard_map/transpose | solution.py:114
  77.4 0.0 slice-start
  77.4 0.0 slice-start.1
  77.5 1.9 %bitcast_reduce_fusion = (f32[2,1024]{1,0:T(2,128)S(1)}, f32[2,1024,1024]{2,1,0:T(8,128)S(1)}) fusion(pred[1024]{0:T(1024)(128)(4,1)S(1)} %broadcast_bitcast_fusion.1, bf16[2,1024,128]{2,1,0:T(8,128)(2,1)S(1)} %bitcast.93, bf16[2,1024,256]{2,1,0:T(8,128)(2,1)S(1)} %bitcast.89), kind=kOutput, calls=%fused_computation.3 | convolution fusion | flops 543160320 | bytes 9446400 | tf_op jit(solution)/shard_map/gqd,gkd->gqk/dot_general | solution.py:14
  79.4 2.5 %fusion.2 = f32[2,1024]{1,0:T(2,128)S(1)} fusion(f32[2,1024,1024]{2,1,0:T(8,128)S(1)} %get-tuple-element.18, f32[2,1024]{1,0:T(2,128)S(1)} %get-tuple-element.13, pred[1024]{0:T(1024)(128)(4,1)S(1)} %broadcast_bitcast_fusion.1), kind=kLoop, calls=%fused_computation.9 | loop fusion | flops 10483712 | bytes 8406016 | tf_op jit(solution)/shard_map/reduce_sum | solution.py:20
  81.9 0.0 slice-done
  81.9 0.0 slice-done.1
  81.9 1.7 %fusion.5 = f32[2,1024]{1,0:T(2,128)S(1)} fusion(f32[2,768,1024]{2,1,0:T(8,128)S(1)} %bitcast.88, f32[2,1024]{1,0:T(2,128)S(1)} %get-tuple-element.14, pred[1024,768]{0,1:T(8,128)(4,1)S(1)} %pad_add_fusion), kind=kLoop, calls=%fused_computation.12 | loop fusion | flops 7862272 | bytes 7094272 | tf_op jit(solution)/shard_map/reduce_sum | solution.py:20
  83.6 2.8 %fusion.20 = f32[2,1024,128]{2,1,0:T(8,128)S(1)} fusion(f32[2,768,1024]{2,1,0:T(8,128)S(1)} %bitcast.88, f32[2,1024]{1,0:T(2,128)S(1)} %get-tuple-element.14, pred[1024,768]{0,1:T(8,128)(4,1)S(1)} %pad_add_fusion, f32[2,1024]{1,0:T(2,128)S(1)} %get-tuple-element.6, f32[2,1024]{1,0:T(2,128)S(1)} %get-tuple-element.12, ...), kind=kOutput, calls=%fused_computation.22 | convolution fusion | flops 411828224 | bytes 8937472 | tf_op jit(solution)/shard_map/gqk,gkd->gqd/dot_general | solution.py:21
  86.4 3.0 %divide_convert_fusion = bf16[2,1024,128]{2,1,0:T(8,128)(2,1)S(1)} fusion(f32[2,1024,128]{2,1,0:T(8,128)S(1)} %fusion.20, f32[2,1024,1024]{2,1,0:T(8,128)S(1)} %get-tuple-element.18, f32[2,1024]{1,0:T(2,128)S(1)} %get-tuple-element.13, pred[1024]{0:T(1024)(128)(4,1)S(1)} %broadcast_bitcast_fusion.1, bf16[2,1024,256]{2,1,0:T(8,128)(2,1)S(1)} %bitcast.90, ...), kind=kOutput, calls=%fused_computation.24 | convolution fusion | flops 548143104 | bytes 10504192 | tf_op jit(solution)/shard_map/gqk,gkd->gqd/dot_general | solution.py:21
  89.4 0.3 copy.29
  89.8 0.9 copy.35
  (21 shorter events, 0.2 us)
Async XLA Ops:
  6.5 16.8 %copy-start.1 = (s32[4]{0:T(128)S(1)}, s32[4]{0:T(128)}, u32[]{:S(2)}) copy-start(s32[4]{0:T(128)} %param.9) | copy-start | bytes 52
  6.5 15.6 %copy-start = (bf16[128,2048]{1,0:T(8,128)(2,1)S(1)}, bf16[128,2048]{1,0:T(8,128)(2,1)}, u32[]{:S(2)}) copy-start(bf16[128,2048]{1,0:T(8,128)(2,1)} %param.5) | copy-start | bytes 1572868
  15.5 32.0 %all-to-all-start = ((bf16[4,2,256,256]{3,2,1,0:T(8,128)(2,1)}), bf16[4,2,256,256]{3,2,1,0:T(8,128)(2,1)S(1)}, u32[]{:S(2)}, u32[]{:S(2)}) async-start(bf16[4,2,256,256]{3,2,1,0:T(8,128)(2,1)} %pad_maximum_fusion), calls=%async_computation | async-start | bytes 2097152 | tf_op jit(solution)/shard_map/all_to_all | solution.py:67
  21.8 54.3 %all-gather.3.cloned.1.call-start = ((), (), s32[]{:S(2)}) async-start(), calls=%async_computation.1 | async-start | bytes 1310720 | tf_op jit(solution)/shard_map/all_gather | solution.py:82
  77.4 4.5 %slice-start = ((s8[6291456]{0:T(1024)(128)(4,1)}), s8[4194304]{0:T(1024)(128)(4,1)S(1)}, s32[]{:S(2)}) async-start(s8[6291456]{0:T(1024)(128)(4,1)} %bitcast.87), calls=%async_computation.2 | async-start | bytes 8388608
  77.4 4.5 %slice-start.1 = ((s8[6291456]{0:T(1024)(128)(4,1)}), s8[2097152]{0:T(1024)(128)(4,1)S(1)}, s32[]{:S(2)}) async-start(s8[6291456]{0:T(1024)(128)(4,1)} %bitcast.87), calls=%async_computation.3 | async-start | bytes 4194304
Sparse Core Ops, SparseCore 0:
  49.1 27.0 all-gather.2
where the time goes:
time: 97.9 us; the launch traced here: 97.5 us
  waiting for transfers between devices  45.4 us (46%)
  between operations  14.3 us (15%)
  matrix products  11.7 us (12%)
  other arithmetic  10.6 us (11%)
  local copies, waits for them, and re-layouts  9.17 us (9%)
  starting transfers between devices  6.32 us (6%)
    all_to_all x1, waiting for transfers between devices, local(): lax.all_to_all(payload, 'blk', split_axis=0, concat_axis=0, tiled=True)  24.1 us
    all_gather x1, waiting for transfers between devices, local(): gathered = lax.all_gather(compact, 'blk', axis=0, tiled=True)  21.3 us
    all_to_all x1, starting transfers between devices, local(): lax.all_to_all(payload, 'blk', split_axis=0, concat_axis=0, tiled=True)  6.32 us
    dot_general x2, matrix products, attend(): jnp.einsum('gqd,gkd->gqk', queries, keys, preferred_element_type=jnp.floa...  5.92 us
    dot_general x2, matrix products, attend(): jnp.einsum('gqk,gkd->gqd', weights.astype(jnp.bfloat16), values, preferre...  5.81 us
    reduce_sum x2, other arithmetic, attend(): totals = totals * factor + jnp.sum(weights, axis=2)  4.16 us
    gather x1, local copies, waits for them, and re-layouts, local(): kv_cache[chosen]  2.77 us
  transfers between devices with their start and end apart: 2, of which 2 were waited for; matrix products, arithmetic and copies ran while one was open for 7% of the time, Pallas kernels for 0%

commit v1 on v0

--- a/solution.py
+++ b/solution.py
@@ -64,7 +64,19 @@
         kv_new.transpose(1, 0, 2)[None], (blocks, kv_heads, q_rows, 2 * head_size)
     )
     payload = jnp.concatenate([sent_pages, own_rows], axis=2)
-    received = lax.all_to_all(payload, "blk", split_axis=0, concat_axis=0, tiled=True)
+    ways, here = (lax.axis_size("blk"), lax.axis_index("blk"))
+    width = payload.shape[0] // ways
+    shape = list(payload.shape)
+    shape[0] = width
+    height = shape[0]
+    shape[0] = height * ways
+    full = jnp.zeros(shape, payload.dtype)
+    for mask in range(ways):
+        part = lax.dynamic_slice_in_dim(payload, (here ^ mask) * width, width, axis=0)
+        if mask:
+            part = lax.ppermute(part, "blk", [(d, d ^ mask) for d in range(ways)])
+        full = lax.dynamic_update_slice_in_dim(full, part, (here ^ mask) * height, axis=0)
+    received = full
     page_part = received[:, :, : per_peer * page_len]
     page_part = page_part.reshape(blocks, kv_heads, per_peer, page_len, 2 * head_size)
     page_part = page_part.transpose(0, 2, 1, 3, 4).reshape(

time: 97.9 us -> 94 us (0.960)
  waiting for transfers between devices: 45.4 us -> 40.6 us
  local copies, waits for them, and re-layouts: 9.17 us -> 10.3 us
    all_to_all x1 -> x0, waiting for transfers between devices: 24.1 us -> none  [local(): lax.all_to_all(payload, 'blk', split_axis=0, concat_axis=0, tiled=True)]
    ppermute x0 -> x3, waiting for transfers between devices: none -> 18.3 us  [local(): part = lax.ppermute(part, 'blk', [(d, d ^ mask) for d in range(ways)])]
    all_to_all x1 -> x0, starting transfers between devices: 6.32 us -> none  [local(): lax.all_to_all(payload, 'blk', split_axis=0, concat_axis=0, tiled=True)]
    ppermute x0 -> x3, starting transfers between devices: none -> 5.76 us  [local(): part = lax.ppermute(part, 'blk', [(d, d ^ mask) for d in range(ways)])]
    select_n x1, other arithmetic: 0.7 us -> 2.02 us  [local(): wanted = (block_ids[:, None] - my_start) % blocks + peer_slots * blocks]
    unnamed x10 -> x6, local copies, waits for them, and re-layouts: 1.06 us -> 2.09 us
    all_gather x1, waiting for transfers between devices: 21.3 us -> 22.3 us  [local(): gathered = lax.all_gather(compact, 'blk', axis=0, tiled=True)]
  transfers between devices with their start and end apart: 2 -> 4, of which waited for: 2 -> 3; matrix products, arithmetic and copies ran while one was open for 7% -> 9% of each run, Pallas kernels for 0% -> 0%
where the time goes in v1:
time: 94 us; the launch traced here: 93.6 us
  waiting for transfers between devices  40.6 us (43%)
  between operations  14.3 us (15%)
  matrix products  11.7 us (12%)
  other arithmetic  10.8 us (11%)
  local copies, waits for them, and re-layouts  10.3 us (11%)
  starting transfers between devices  5.76 us (6%)
    all_gather x1, waiting for transfers between devices, local(): gathered = lax.all_gather(compact, 'blk', axis=0, tiled=True)  22.3 us
    ppermute x3, waiting for transfers between devices, local(): part = lax.ppermute(part, 'blk', [(d, d ^ mask) for d in range(ways)])  18.3 us
    dot_general x2, matrix products, attend(): jnp.einsum('gqd,gkd->gqk', queries, keys, preferred_element_type=jnp.floa...  5.92 us
    dot_general x2, matrix products, attend(): jnp.einsum('gqk,gkd->gqd', weights.astype(jnp.bfloat16), values, preferre...  5.81 us
    ppermute x3, starting transfers between devices, local(): part = lax.ppermute(part, 'blk', [(d, d ^ mask) for d in range(ways)])  5.76 us
    reduce_sum x2, other arithmetic, attend(): totals = totals * factor + jnp.sum(weights, axis=2)  4.16 us
    gather x1, local copies, waits for them, and re-layouts, local(): kv_cache[chosen]  2.77 us
    unnamed x6, local copies, waits for them, and re-layouts  2.09 us
  transfers between devices with their start and end apart: 4, of which 3 were waited for; matrix products, arithmetic and copies ran while one was open for 9% of the time, Pallas kernels for 0%

profile of v1, /device:TPU:0, one launch (start us, length us, event | category | flops | bytes accessed | tf_op | source)
XLA Modules:
  0.0 93.6 jit_solution(13628126423432896177)
XLA Ops:
  6.5 0.0 all-gather.3.cloned.1.call-start
  6.5 0.7 and_select_fusion.3
  7.2 0.7 convert_bitcast_fusion
  7.9 0.2 reduce-window.21
  8.1 0.1 convert_reduce_fusion
  8.2 0.2 reduce-window.22
  8.4 0.6 fusion.41
  9.0 2.0 %and_select_fusion.4 = (s32[4]{0:T(128)S(1)}, s32[]{:T(128)}) fusion(s32[]{:T(128)} %fusion.41, s32[4]{0:T(128)} %param.9, s32[]{:T(128)S(6)} %axis_index.19), kind=kLoop, calls=%fused_computation.82 | loop fusion | flops 59 | bytes 44 | tf_op jit(solution)/shard_map/jit(remainder)/select_n | solution.py:56
  11.0 0.2 select_reduce_fusion.1
  11.2 0.9 copy.31
  12.2 2.8 %gather_fusion = bf16[4,2,128,256]{3,2,1,0:T(8,128)(2,1)S(1)} fusion(bf16[32,2,128,256]{3,2,1,0:T(8,128)(2,1)} %param.7, s32[1024]{0:T(1024)S(1)} %pad_clamp_fusion.1), kind=kCustom, calls=%fused_computation | custom fusion | bytes 1048592 | tf_op jit(solution)/shard_map/gather | solution.py:59
  15.0 0.1 broadcast_in_dim.150
  15.1 0.1 fusion.32
  15.1 5.1 %collective-permute-start.2 = (bf16[1,2,256,256]{3,2,1,0:T(8,128)(2,1)S(1)}, bf16[1,2,256,256]{3,2,1,0:T(8,128)(2,1)S(1)}, u32[]{:S(2)}, u32[]{:S(2)}) collective-permute-start(bf16[1,2,256,256]{3,2,1,0:T(8,128)(2,1)S(1)} %get-tuple-element.12), channel_id=1, source_target_pairs={{0,12},{4,8},{8,4},{12,0},{1,13},{5,9},{9,5},{13,1},{2,14},{6,10},... | collective-permute-start | bytes 786440 | tf_op jit(solution)/shard_map/ppermute | solution.py:77
  20.3 0.0 collective-permute-start
  20.3 0.6 collective-permute-start.1
  21.0 0.1 broadcast_bitcast_fusion.2
  21.0 0.2 reduce-window.23
  21.2 0.1 fusion.38
  21.4 0.7 select_reduce_fusion
  22.8 0.1 and.99
  22.9 1.1 %copy.41 = bf16[16,8,16,128]{3,2,1,0:T(8,128)(2,1)S(1)} copy(bf16[16,8,16,128]{3,1,2,0:T(8,128)(2,1)} %bitcast.97) | data formatting | bytes 1048576
  24.1 0.1 copy.34
  24.2 9.1 %collective-permute-done = bf16[1,2,256,256]{3,2,1,0:T(8,128)(2,1)S(1)} collective-permute-done((bf16[1,2,256,256]{3,2,1,0:T(8,128)(2,1)S(1)}, bf16[1,2,256,256]{3,2,1,0:T(8,128)(2,1)S(1)}, u32[]{:S(2)}, u32[]{:S(2)}) %collective-permute-start) | collective-permute-done | bytes 262176 | tf_op jit(solution)/shard_map/ppermute | solution.py:77
  33.3 9.2 %collective-permute-done.1 = bf16[1,2,256,256]{3,2,1,0:T(8,128)(2,1)S(1)} collective-permute-done((bf16[1,2,256,256]{3,2,1,0:T(8,128)(2,1)S(1)}, bf16[1,2,256,256]{3,2,1,0:T(8,128)(2,1)S(1)}, u32[]{:S(2)}, u32[]{:S(2)}) %collective-permute-start.1) | collective-permute-done | bytes 262176 | tf_op jit(solution)/shard_map/ppermute | solution.py:77
  42.6 0.0 collective-permute-done.2
  42.6 0.1 fusion.56
  42.7 1.3 %gather_fusion.1 = bf16[2,2,128,256]{3,2,1,0:T(8,128)(2,1)} fusion(bf16[4,2,128,256]{3,2,1,0:T(8,128)(2,1)S(1)} %get-tuple-element.10, s32[1024]{0:T(1024)S(1)} %pad_clamp_fusion), kind=kCustom, calls=%fused_computation.1 | custom fusion | bytes 524296 | tf_op jit(solution)/shard_map/gather | solution.py:92
  44.0 0.0 all-gather.3.cloned.1.call-update
  44.0 0.1 broadcast_bitcast_fusion.1
  44.1 0.4 broadcast_compare_fusion
  44.5 0.4 pad_add_fusion
  44.9 1.0 %copy.33 = bf16[2,2,128,256]{3,2,1,0:T(8,128)(2,1)S(1)} copy(bf16[2,2,128,256]{3,2,0,1:T(8,128)(2,1)} %bitcast.91) | data formatting | bytes 524288 | tf_op jit(solution)/shard_map/transpose | solution.py:100
  45.9 4.0 %fusion.4 = (f32[2,1024]{1,0:T(2,128)S(1)}, f32[2,768,1024]{2,1,0:T(8,128)}) fusion(pred[1024,768]{0,1:T(8,128)(4,1)S(1)} %pad_add_fusion, bf16[2,1024,128]{2,1,0:T(8,128)(2,1)S(1)} %bitcast.92, bf16[2,512,256]{2,1,0:T(8,128)(2,1)S(1)} %bitcast.98, bf16[2,256,256]{2,1,0:T(8,128)(2,1)S(1)} %bitcast.101), kind=kOutput, calls=%fused_computation.11 | convolution fusion | flops 408156160 | bytes 8396800 | tf_op jit(solution)/shard_map/gqd,gkd->gqk/dot_general | solution.py:14
  49.9 22.3 %all-gather.3.cloned.1.call-done = bf16[8,2,128,256]{3,2,1,0:T(8,128)(2,1)} async-done(((bf16[2,2,128,256]{3,2,1,0:T(8,128)(2,1)}), bf16[8,2,128,256]{3,2,1,0:T(8,128)(2,1)}) %all-gather.3.cloned.1.call-update) | async-done | bytes 1048592 | tf_op jit(solution)/shard_map/all_gather | solution.py:94
  72.2 1.3 %copy.36 = bf16[2,8,128,256]{3,2,1,0:T(8,128)(2,1)S(1)} copy(bf16[2,8,128,256]{3,2,0,1:T(8,128)(2,1)} %bitcast.96) | data formatting | bytes 2097152 | tf_op jit(solution)/shard_map/transpose | solution.py:126
  73.5 0.0 slice-start
  73.5 0.0 slice-start.1
  73.6 1.9 %bitcast_reduce_fusion = (f32[2,1024]{1,0:T(2,128)S(1)}, f32[2,1024,1024]{2,1,0:T(8,128)S(1)}) fusion(pred[1024]{0:T(1024)(128)(4,1)S(1)} %broadcast_bitcast_fusion.1, bf16[2,1024,128]{2,1,0:T(8,128)(2,1)S(1)} %bitcast.93, bf16[2,1024,256]{2,1,0:T(8,128)(2,1)S(1)} %bitcast.89), kind=kOutput, calls=%fused_computation.3 | convolution fusion | flops 543160320 | bytes 9446400 | tf_op jit(solution)/shard_map/gqd,gkd->gqk/dot_general | solution.py:14
  75.5 2.5 %fusion.2 = f32[2,1024]{1,0:T(2,128)S(1)} fusion(f32[2,1024,1024]{2,1,0:T(8,128)S(1)} %get-tuple-element.22, f32[2,1024]{1,0:T(2,128)S(1)} %get-tuple-element.17, pred[1024]{0:T(1024)(128)(4,1)S(1)} %broadcast_bitcast_fusion.1), kind=kLoop, calls=%fused_computation.9 | loop fusion | flops 10483712 | bytes 8406016 | tf_op jit(solution)/shard_map/reduce_sum | solution.py:20
  78.0 0.0 slice-done
  78.0 0.0 slice-done.1
  78.0 1.7 %fusion.5 = f32[2,1024]{1,0:T(2,128)S(1)} fusion(f32[2,768,1024]{2,1,0:T(8,128)S(1)} %bitcast.88, f32[2,1024]{1,0:T(2,128)S(1)} %get-tuple-element.18, pred[1024,768]{0,1:T(8,128)(4,1)S(1)} %pad_add_fusion), kind=kLoop, calls=%fused_computation.12 | loop fusion | flops 7862272 | bytes 7094272 | tf_op jit(solution)/shard_map/reduce_sum | solution.py:20
  79.7 2.8 %fusion.20 = f32[2,1024,128]{2,1,0:T(8,128)S(1)} fusion(f32[2,768,1024]{2,1,0:T(8,128)S(1)} %bitcast.88, f32[2,1024]{1,0:T(2,128)S(1)} %get-tuple-element.18, pred[1024,768]{0,1:T(8,128)(4,1)S(1)} %pad_add_fusion, f32[2,1024]{1,0:T(2,128)S(1)} %get-tuple-element.6, f32[2,1024]{1,0:T(2,128)S(1)} %get-tuple-element.16, ...), kind=kOutput, calls=%fused_computation.30 | convolution fusion | flops 411828224 | bytes 8937472 | tf_op jit(solution)/shard_map/gqk,gkd->gqd/dot_general | solution.py:21
  82.5 3.0 %divide_convert_fusion = bf16[2,1024,128]{2,1,0:T(8,128)(2,1)S(1)} fusion(f32[2,1024,128]{2,1,0:T(8,128)S(1)} %fusion.20, f32[2,1024,1024]{2,1,0:T(8,128)S(1)} %get-tuple-element.22, f32[2,1024]{1,0:T(2,128)S(1)} %get-tuple-element.17, pred[1024]{0:T(1024)(128)(4,1)S(1)} %broadcast_bitcast_fusion.1, bf16[2,1024,256]{2,1,0:T(8,128)(2,1)S(1)} %bitcast.90, ...), kind=kOutput, calls=%fused_computation.31 | convolution fusion | flops 548143104 | bytes 10504192 | tf_op jit(solution)/shard_map/gqk,gkd->gqd/dot_general | solution.py:21
  85.5 0.3 copy.38
  85.9 0.9 copy.44
  (24 shorter events, 0.3 us)
Async XLA Ops:
  6.5 65.7 %all-gather.3.cloned.1.call-start = ((), (), s32[]{:S(2)}) async-start(), calls=%async_computation | async-start | bytes 1310720 | tf_op jit(solution)/shard_map/all_gather | solution.py:94
  15.1 27.5 %collective-permute-start.2 = (bf16[1,2,256,256]{3,2,1,0:T(8,128)(2,1)S(1)}, bf16[1,2,256,256]{3,2,1,0:T(8,128)(2,1)S(1)}, u32[]{:S(2)}, u32[]{:S(2)}) collective-permute-start(bf16[1,2,256,256]{3,2,1,0:T(8,128)(2,1)S(1)} %get-tuple-element.12), channel_id=1, source_target_pairs={{0,12},{4,8},{8,4},{12,0},{1,13},{5,9},{9,5},{13,1},{2,14},{6,10},... | collective-permute-start | bytes 786440 | tf_op jit(solution)/shard_map/ppermute | solution.py:77
  20.3 13.1 %collective-permute-start = (bf16[1,2,256,256]{3,2,1,0:T(8,128)(2,1)S(1)}, bf16[1,2,256,256]{3,2,1,0:T(8,128)(2,1)S(1)}, u32[]{:S(2)}, u32[]{:S(2)}) collective-permute-start(bf16[1,2,256,256]{3,2,1,0:T(8,128)(2,1)S(1)} %get-tuple-element.14), channel_id=1, source_target_pairs={{0,4},{4,0},{8,12},{12,8},{1,5},{5,1},{9,13},{13,9},{2,6},{6,2},{1... | collective-permute-start | bytes 786440 | tf_op jit(solution)/shard_map/ppermute | solution.py:77
  20.3 22.3 %collective-permute-start.1 = (bf16[1,2,256,256]{3,2,1,0:T(8,128)(2,1)S(1)}, bf16[1,2,256,256]{3,2,1,0:T(8,128)(2,1)S(1)}, u32[]{:S(2)}, u32[]{:S(2)}) collective-permute-start(bf16[1,2,256,256]{3,2,1,0:T(8,128)(2,1)S(1)} %get-tuple-element.15), channel_id=1, source_target_pairs={{0,8},{4,12},{8,0},{12,4},{1,9},{5,13},{9,1},{13,5},{2,10},{6,14},... | collective-permute-start | bytes 786440 | tf_op jit(solution)/shard_map/ppermute | solution.py:77
  73.5 4.5 %slice-start = ((s8[6291456]{0:T(1024)(128)(4,1)}), s8[4194304]{0:T(1024)(128)(4,1)S(1)}, s32[]{:S(2)}) async-start(s8[6291456]{0:T(1024)(128)(4,1)} %bitcast.87), calls=%async_computation.1 | async-start | bytes 8388608
  73.5 4.5 %slice-start.1 = ((s8[6291456]{0:T(1024)(128)(4,1)}), s8[2097152]{0:T(1024)(128)(4,1)S(1)}, s32[]{:S(2)}) async-start(s8[6291456]{0:T(1024)(128)(4,1)} %bitcast.87), calls=%async_computation.2 | async-start | bytes 4194304
Sparse Core Ops, SparseCore 0:
  44.1 28.0 all-gather.2
